TPU v7x, 512 devices: a whole 4x4x16 slice. The times are simulated.
512 devices in a mesh: dp: 64 (over z, x), pair: 8 (over y, core).
Axes of the slice: x: 4, y: 4, z: 16, core: 2. Of those that a mesh axis runs over, the one named last changes fastest.
Arguments:
- embedding: bfloat16 [65536, 1024], P(('dp', 'pair')), may hold values from -32 to 32
- labels: int32 [65536], P(('dp', 'pair')), may hold values from 0 to 127, as said below
- order_ids: int32 [65536], P(('dp', 'pair')), may hold values from 0 to 65535, each once
Outputs:
- best_similarity: float32 [65536], P(('dp', 'pair'))
Inputs may be any that keep to these rules, and one draw needn't show every extreme that they name: `labels`: clusters 2 * g to 2 * g + 1 form owner group g. Among the 128 rows of one device (aligned blocks of the whole array) at most 4 name clusters of any one group, and in every draw some group gets exactly 4 rows from every device.
All inputs are finite; a program needn't handle non-finite values.
Results may differ from a plain program's by a relative error of at most 0.00049.
Values may be sent and summed in bfloat16 or wider, within the bound.
No kernel may reach another device: no remote copies, remote signals or barrier semaphores. Data moves between devices by JAX's collectives and lax.ppermute only.
A program may use at most 64 MiB of HBM per device.

v0:
```python
import jax
import jax.numpy as jnp
from jax import lax
from jax.sharding import PartitionSpec as P

CL_OWN = 2
META = 128
PUBLISH_ROWS = 32


def tile_best(own_rows, own_key, other_rows, other_key, rows_total):
    scores = jnp.dot(own_rows, other_rows.T, preferred_element_type=jnp.float32)
    same_cluster = other_key[None, :] // rows_total == own_key[:, None] // rows_total
    earlier = same_cluster & (other_key[None, :] < own_key[:, None])
    return jnp.max(jnp.where(earlier, scores, -1.0), axis=1)


def slot_keys(rows, width, rows_total):
    meta = rows[:, width : width + 3].astype(jnp.int32)
    return meta[:, 0] * rows_total + meta[:, 1] * 256 + meta[:, 2]


def on_device(embedding, labels, order_ids):
    groups = lax.axis_size("dp")
    pairs = lax.axis_size("pair")
    rows_here, width = embedding.shape
    rows_total = rows_here * groups * pairs
    capacity = 2 * rows_here // groups
    slot_count = groups * capacity
    values = embedding.astype(jnp.float32)
    squares = jnp.sum(values * values, axis=1, keepdims=True)
    shifted = squares + 1e-06
    unit_rows = (values * lax.rsqrt(shifted)).astype(jnp.bfloat16)
    owner_group = labels // CL_OWN
    onehot = (owner_group[:, None] == jnp.arange(groups, dtype=jnp.int32)[None, :]).astype(
        jnp.int32
    )
    before = jnp.cumsum(onehot, axis=0) - onehot
    slot_index = owner_group * capacity + jnp.sum(before * onehot, axis=1)
    meta = jnp.stack([labels + 1, order_ids // 256, order_ids % 256], axis=1).astype(jnp.bfloat16)
    meta = jnp.pad(meta, ((0, 0), (0, META - 3)))
    packed = jnp.concatenate([unit_rows, meta], axis=1)
    send_rows = jnp.zeros((slot_count, width + META), jnp.bfloat16).at[slot_index].set(packed)
    got_rows = lax.all_to_all(
        send_rows.reshape(groups, capacity, -1), "dp", split_axis=0, concat_axis=0, tiled=True
    ).reshape(slot_count, -1)
    piece_rows = lax.all_gather(got_rows, "pair", axis=0, tiled=True)
    got_key = slot_keys(got_rows, width, rows_total)
    piece_key = slot_keys(piece_rows, width, rows_total)
    column = lax.broadcasted_iota(jnp.int32, got_rows.shape, 1)
    query_rows = jnp.where(column < width, got_rows, jnp.zeros_like(got_rows))
    best_seen = jnp.full((slot_count,), -1.0, jnp.float32)
    piece_count = piece_rows.shape[0]
    for offset in range(0, piece_count, 512):
        width_now = min(512, piece_count - offset)
        found = tile_best(
            query_rows,
            got_key,
            piece_rows[offset : offset + width_now],
            piece_key[offset : offset + width_now],
            rows_total,
        )
        best_seen = jnp.maximum(best_seen, found)
    publish = jnp.zeros((PUBLISH_ROWS * 128,), jnp.float32).at[:slot_count].set(best_seen)
    published = lax.all_gather(publish.reshape(PUBLISH_ROWS, 128), "dp", axis=0, tiled=False)
    me = lax.axis_index("dp")
    answered = lax.dynamic_slice_in_dim(
        published.reshape(groups, PUBLISH_ROWS * 128), me * capacity, capacity, axis=1
    )
    return answered.reshape(slot_count)[slot_index]


def solution(mesh):
    in_specs = (P(("dp", "pair"), None), P(("dp", "pair")), P(("dp", "pair")))
    out_specs = P(("dp", "pair"))
    return jax.shard_map(
        on_device, mesh=mesh, in_specs=in_specs, out_specs=out_specs, check_vma=False
    )
```

profile of v0, /device:TPU:8, one launch (start us, length us, event | category | flops | bytes accessed | tf_op | source)
XLA Modules:
  0.0 256.4 jit_solution(14375752796550664068)
XLA Ops:
  6.5 0.7 convert_bitcast_fusion.1
  7.3 0.2 reduce_window_sum.11
  7.5 0.2 select_reduce_fusion
  7.7 0.7 convert_bitcast_fusion
  8.5 1.1 fusion.18
  9.6 1.1 fusion.19
  10.6 1.3 scatter_custom_fusion
  12.1 54.0 %all_to_all.5 = bf16[64,4,1152]{2,1,0:T(4,128)(2,1)S(1)} all-to-all(bf16[64,4,1152]{2,1,0:T(4,128)(2,1)S(1)} %reshape.149), channel_id=1, replica_groups=mesh['dp'=64,'pair'=8] {'dp'}, dimensions={0} | all-to-all | bytes 1179648 | tf_op jit(solution)/shard_map/all_to_all | solution.py:44
  66.1 1.0 reshape.150
  67.2 0.9 slice_convert_fusion.1
  68.1 0.3 fusion.33
  68.4 31.6 %all-gather.3.cloned.1.call-done = bf16[2048,1152]{1,0:T(8,128)(2,1)} async-done(((bf16[256,1152]{1,0:T(8,128)(2,1)}), bf16[2048,1152]{1,0:T(8,128)(2,1)}) %all-gather.3.cloned.1.call-update) | async-done | bytes 4718608 | tf_op jit(solution)/shard_map/all_gather | solution.py:47
  99.9 1.3 slice_convert_fusion
  101.2 0.6 slice_add_fusion
  101.8 0.4 slice_reduce_fusion.3
  102.2 0.2 copy-done.1
  102.4 0.6 fusion.4
  103.1 0.6 fusion.7
  103.7 0.6 fusion.10
  104.4 0.6 fusion.13
  105.0 0.6 pad_bitcast_fusion
  105.7 140.1 %all-gather.5.cloned.1.call-done = f32[64,32,128]{2,1,0:T(8,128)} async-done(((f32[1,32,128]{2,1,0:T(8,128)}), f32[64,32,128]{2,1,0:T(8,128)}) %all-gather.5.cloned.1.call-update) | async-done | bytes 1048592 | tf_op jit(solution)/shard_map/all_gather | solution.py:65
  245.8 1.8 copy.10
  247.8 1.8 gather_fusion
  (20 shorter events, 0.7 us)
Async XLA Ops:
  6.5 93.4 %all-gather.3.cloned.1.call-start = ((), (), s32[]{:S(2)}) async-start(), calls=%async_computation.1 | async-start | bytes 5308416 | tf_op jit(solution)/shard_map/all_gather | solution.py:47
  67.1 35.1 %copy-start = (bf16[256,1152]{1,0:T(8,128)(2,1)S(1)}, bf16[256,1152]{1,0:T(8,128)(2,1)}, u32[]{:S(2)}) copy-start(bf16[256,1152]{1,0:T(8,128)(2,1)} %reshape.150) | copy-start | bytes 1769476
  67.1 178.7 %all-gather.5.cloned.1.call-start = ((), (), s32[]{:S(2)}) async-start(), calls=%async_computation.2 | async-start | bytes 1064960 | tf_op jit(solution)/shard_map/all_gather | solution.py:65
  99.9 2.5 copy-start.1
Sparse Core Ops, SparseCore 0:
  67.2 32.6 all-gather.2
  105.8 139.9 all-gather.4
where the time goes:
time: 257 us; the launch traced here: 256 us
  waiting for transfers between devices  172 us (67%)
  blocking collectives  54 us (21%)
  between operations  13.5 us (5%)
  other arithmetic  8.4 us (3%)
  local copies, waits for them, and re-layouts  6.2 us (2%)
    all_gather x1, waiting for transfers between devices, on_device(): lax.all_gather(publish.reshape(PUBLISH_ROWS, 128), 'dp', axis=0, tiled=Fa...  140 us
    all_to_all x1, blocking collectives, on_device(): lax.all_to_all(send_rows.reshape(groups, capacity, -1), 'dp', split_axis=...  54 us
    all_gather x1, waiting for transfers between devices, on_device(): piece_rows = lax.all_gather(got_rows, 'pair', axis=0, tiled=True)  31.6 us
  transfers between devices with their start and end apart: 2, of which 2 were waited for; matrix products, arithmetic and copies ran while one was open for 0% of the time, Pallas kernels for 0%

commit v1 on v0

--- a/solution.py
+++ b/solution.py
@@ -44,7 +44,27 @@
     got_rows = lax.all_to_all(
         send_rows.reshape(groups, capacity, -1), "dp", split_axis=0, concat_axis=0, tiled=True
     ).reshape(slot_count, -1)
-    piece_rows = lax.all_gather(got_rows, "pair", axis=0, tiled=True)
+    front = jax.lax.axis_size("pair")
+    p_next = jax.lax.axis_index("pair")
+    seen_now, small, far_arr = (front, p_next, got_rows.shape[0])
+    lanes = [(d, (d + 1) % seen_now) for d in range(seen_now)]
+    ledger = [(d, (d - 1) % seen_now) for d in range(seen_now)]
+    piece_rows = jnp.zeros(
+        (*got_rows.shape[:0], seen_now * far_arr, *got_rows.shape[1:]), got_rows.dtype
+    )
+    piece_rows = lax.dynamic_update_slice_in_dim(piece_rows, got_rows, small * far_arr, axis=0)
+    next_value = passed = got_rows
+    heard = seen_now // 2
+    for m in tuple(range(1, heard + 1)):
+        next_value = jax.lax.ppermute(next_value, "pair", lanes)
+        piece_rows = lax.dynamic_update_slice_in_dim(
+            piece_rows, next_value, (small - m) % seen_now * far_arr, axis=0
+        )
+        if m < seen_now - heard:
+            passed = jax.lax.ppermute(passed, "pair", ledger)
+            piece_rows = lax.dynamic_update_slice_in_dim(
+                piece_rows, passed, (small + m) % seen_now * far_arr, axis=0
+            )
     got_key = slot_keys(got_rows, width, rows_total)
     piece_key = slot_keys(piece_rows, width, rows_total)
     column = lax.broadcasted_iota(jnp.int32, got_rows.shape, 1)

time: 257 us -> 258 us (level)
  waiting for transfers between devices: 172 us -> 153 us
  local copies, waits for them, and re-layouts: 6.2 us -> 17.7 us
  starting transfers between devices: 0.04 us -> 5.3 us
  matrix products: 2.55 us -> 7.48 us
    all_gather x1 -> x0, waiting for transfers between devices: 31.6 us -> none  [on_device(): piece_rows = lax.all_gather(got_rows, 'pair', axis=0, tiled=True)]
    ppermute x0 -> x7, waiting for transfers between devices: none -> 19.8 us  [the longest x4 19.8 us: on_device(): next_value = jax.lax.ppermute(next_value, 'pair', lanes)]
    dynamic_update_slice x0 -> x8, local copies, waits for them, and re-layouts: none -> 7.19 us  [the longest x4 3.63 us: on_device(): lax.dynamic_update_slice_in_dim(piece_rows, next_value, (small - m) % see...]
    all_gather x1, waiting for transfers between devices: 140 us -> 133 us  [on_device(): lax.all_gather(publish.reshape(PUBLISH_ROWS, 128), 'dp', axis=0, tiled=Fa...]
    ppermute x0 -> x7, starting transfers between devices: none -> 5.3 us  [the longest x3 5.28 us: on_device(): passed = jax.lax.ppermute(passed, 'pair', ledger)]
    dot_general x4, matrix products: 2.55 us -> 7.48 us  [tile_best(): scores = jnp.dot(own_rows, other_rows.T, preferred_element_type=jnp.float32)]
    ppermute x0 -> x7, local copies, waits for them, and re-layouts: none -> 2.77 us  [the longest x3 1.79 us: on_device(): passed = jax.lax.ppermute(passed, 'pair', ledger)]
    broadcast_in_dim x0 -> x1, local copies, waits for them, and re-layouts: none -> 2.72 us  [on_device(): jnp.zeros((*got_rows.shape[:0], seen_now * far_arr, *got_rows.shape[1:]),...]
  transfers between devices with their start and end apart: 2 -> 8, of which waited for: 2 -> 5; matrix products, arithmetic and copies ran while one was open for 0% -> 5% of each run, Pallas kernels for 0% -> 0%
where the time goes in v1:
time: 258 us; the launch traced here: 257 us
  waiting for transfers between devices  153 us (59%)
  blocking collectives  54 us (21%)
  local copies, waits for them, and re-layouts  17.7 us (7%)
  between operations  13.6 us (5%)
  matrix products  7.48 us (3%)
  other arithmetic  6.4 us (2%)
  starting transfers between devices  5.3 us (2%)
    all_gather x1, waiting for transfers between devices, on_device(): lax.all_gather(publish.reshape(PUBLISH_ROWS, 128), 'dp', axis=0, tiled=Fa...  133 us
    all_to_all x1, blocking collectives, on_device(): lax.all_to_all(send_rows.reshape(groups, capacity, -1), 'dp', split_axis=...  54 us
    ppermute x4, waiting for transfers between devices, on_device(): next_value = jax.lax.ppermute(next_value, 'pair', lanes)  19.8 us
    dot_general x4, matrix products, tile_best(): scores = jnp.dot(own_rows, other_rows.T, preferred_element_type=jnp.float32)  7.48 us
    ppermute x3, starting transfers between devices, on_device(): passed = jax.lax.ppermute(passed, 'pair', ledger)  5.28 us
  transfers between devices with their start and end apart: 8, of which 5 were waited for; matrix products, arithmetic and copies ran while one was open for 5% of the time, Pallas kernels for 0%

profile of v1, /device:TPU:8, one launch (start us, length us, event | category | flops | bytes accessed | tf_op | source)
XLA Modules:
  0.0 257.2 jit_solution(6511885523954013511)
XLA Ops:
  8.5 1.1 fusion.17
  9.6 1.1 fusion.18
  10.6 1.3 scatter_custom_fusion
  12.1 54.0 %all_to_all.5 = bf16[64,4,1152]{2,1,0:T(4,128)(2,1)S(1)} all-to-all(bf16[64,4,1152]{2,1,0:T(4,128)(2,1)S(1)} %reshape.149), channel_id=1, replica_groups=mesh['dp'=64,'pair'=8] {'dp'}, dimensions={0} | all-to-all | bytes 1179648 | tf_op jit(solution)/shard_map/all_to_all | solution.py:44
  66.3 1.7 collective-permute-start.1
  68.3 7.3 %collective-permute-done = bf16[256,1152]{1,0:T(8,128)(2,1)S(1)} collective-permute-done((bf16[256,1152]{1,0:T(8,128)(2,1)S(1)}, bf16[256,1152]{1,0:T(8,128)(2,1)S(1)}, u32[]{:S(2)}, u32[]{:S(2)}) %collective-permute-start) | collective-permute-done | bytes 589856 | tf_op jit(solution)/shard_map/ppermute | solution.py:59
  75.6 1.8 collective-permute-start.3
  77.7 2.7 %broadcast_in_dim.13 = bf16[2048,1152]{0,1:T(8,128)(2,1)} broadcast(bf16[]{:T(256)} %constant.173.clone.1), dimensions={} | broadcast | bytes 4718594 | tf_op jit(solution)/shard_map/broadcast_in_dim | solution.py:52
  81.5 3.4 %collective-permute-done.2 = bf16[256,1152]{1,0:T(8,128)(2,1)S(1)} collective-permute-done((bf16[256,1152]{1,0:T(8,128)(2,1)S(1)}, bf16[256,1152]{1,0:T(8,128)(2,1)S(1)}, u32[]{:S(2)}, u32[]{:S(2)}) %collective-permute-start.2) | collective-permute-done | bytes 589856 | tf_op jit(solution)/shard_map/ppermute | solution.py:59
  84.9 0.9 constant_dynamic-update-slice_fusion.6
  86.1 1.8 collective-permute-start.5
  87.8 0.9 constant_dynamic-update-slice_fusion.5
  89.2 0.9 constant_dynamic-update-slice_fusion.4
  90.2 4.0 %collective-permute-done.4 = bf16[256,1152]{1,0:T(8,128)(2,1)S(1)} collective-permute-done((bf16[256,1152]{1,0:T(8,128)(2,1)S(1)}, bf16[256,1152]{1,0:T(8,128)(2,1)S(1)}, u32[]{:S(2)}, u32[]{:S(2)}) %collective-permute-start.4) | collective-permute-done | bytes 589856 | tf_op jit(solution)/shard_map/ppermute | solution.py:59
  95.4 1.3 copy.21
  96.7 0.9 constant_dynamic-update-slice_fusion.2
  98.5 5.1 %collective-permute-done.6 = bf16[256,1152]{1,0:T(8,128)(2,1)S(1)} collective-permute-done((bf16[256,1152]{1,0:T(8,128)(2,1)S(1)}, bf16[256,1152]{1,0:T(8,128)(2,1)S(1)}, u32[]{:S(2)}, u32[]{:S(2)}) %collective-permute-start.6) | collective-permute-done | bytes 589856 | tf_op jit(solution)/shard_map/ppermute | solution.py:59
  105.5 1.9 fusion.4
  107.3 1.9 fusion.7
  109.2 1.9 fusion.10
  111.1 1.9 fusion.13
  113.6 133.0 %all-gather.2.cloned.1.call-done = f32[64,32,128]{2,1,0:T(8,128)} async-done(((f32[1,32,128]{2,1,0:T(8,128)}), f32[64,32,128]{2,1,0:T(8,128)}) %all-gather.2.cloned.1.call-update) | async-done | bytes 1048592 | tf_op jit(solution)/shard_map/all_gather | solution.py:85
  246.6 1.8 copy.26
  248.6 1.8 gather_fusion
  (44 shorter events, 9.4 us)
Async XLA Ops:
  6.5 240.1 %all-gather.2.cloned.1.call-start = ((), (), s32[]{:S(2)}) async-start(), calls=%async_computation.1 | async-start | bytes 1064960 | tf_op jit(solution)/shard_map/all_gather | solution.py:85
  66.3 9.3 %collective-permute-start = (bf16[256,1152]{1,0:T(8,128)(2,1)S(1)}, bf16[256,1152]{1,0:T(8,128)(2,1)S(1)}, u32[]{:S(2)}, u32[]{:S(2)}) collective-permute-start(bf16[256,1152]{1,0:T(8,128)(2,1)S(1)} %reshape.150), channel_id=1, source_target_pairs={{0,1},{1,2},{2,3},{3,4},{4,5},{5,6},{6,7},{7,0},{8,9},{9,10},{10,1... | collective-permute-start | bytes 1769480 | tf_op jit(solution)/shard_map/ppermute | solution.py:59
  66.3 9.3 %collective-permute-start.1 = (bf16[256,1152]{1,0:T(8,128)(2,1)S(1)}, bf16[256,1152]{1,0:T(8,128)(2,1)S(1)}, u32[]{:S(2)}, u32[]{:S(2)}) collective-permute-start(bf16[256,1152]{1,0:T(8,128)(2,1)S(1)} %reshape.150), channel_id=1, source_target_pairs={{0,7},{1,0},{2,1},{3,2},{4,3},{5,4},{6,5},{7,6},{8,15},{9,8},{10,9... | collective-permute-start | bytes 1769480 | tf_op jit(solution)/shard_map/ppermute | solution.py:64
  75.6 9.3 %collective-permute-start.2 = (bf16[256,1152]{1,0:T(8,128)(2,1)S(1)}, bf16[256,1152]{1,0:T(8,128)(2,1)S(1)}, u32[]{:S(2)}, u32[]{:S(2)}) collective-permute-start(bf16[256,1152]{1,0:T(8,128)(2,1)S(1)} %collective-permute-done), channel_id=1, source_target_pairs={{0,1},{1,2},{2,3},{3,4},{4,5},{5,6},{6,7},{7,0},{8,9},{9,10},{10,1... | collective-permute-start | bytes 1769480 | tf_op jit(solution)/shard_map/ppermute | solution.py:59
  75.6 10.4 %collective-permute-start.3 = (bf16[256,1152]{1,0:T(8,128)(2,1)S(1)}, bf16[256,1152]{1,0:T(8,128)(2,1)S(1)}, u32[]{:S(2)}, u32[]{:S(2)}) collective-permute-start(bf16[256,1152]{1,0:T(8,128)(2,1)S(1)} %collective-permute-done.1), channel_id=1, source_target_pairs={{0,7},{1,0},{2,1},{3,2},{4,3},{5,4},{6,5},{7,6},{8,15},{9,8},{10,9... | collective-permute-start | bytes 1769480 | tf_op jit(solution)/shard_map/ppermute | solution.py:64
  84.9 9.3 %collective-permute-start.4 = (bf16[256,1152]{1,0:T(8,128)(2,1)S(1)}, bf16[256,1152]{1,0:T(8,128)(2,1)S(1)}, u32[]{:S(2)}, u32[]{:S(2)}) collective-permute-start(bf16[256,1152]{1,0:T(8,128)(2,1)S(1)} %collective-permute-done.2), channel_id=1, source_target_pairs={{0,1},{1,2},{2,3},{3,4},{4,5},{5,6},{6,7},{7,0},{8,9},{9,10},{10,1... | collective-permute-start | bytes 1769480 | tf_op jit(solution)/shard_map/ppermute | solution.py:59
  86.1 9.3 %collective-permute-start.5 = (bf16[256,1152]{1,0:T(8,128)(2,1)S(1)}, bf16[256,1152]{1,0:T(8,128)(2,1)}, u32[]{:S(2)}, u32[]{:S(2)}) collective-permute-start(bf16[256,1152]{1,0:T(8,128)(2,1)S(1)} %collective-permute-done.3), channel_id=1, source_target_pairs={{0,7},{1,0},{2,1},{3,2},{4,3},{5,4},{6,5},{7,6},{8,15},{9,8},{10,9... | collective-permute-start | bytes 1769480 | tf_op jit(solution)/shard_map/ppermute | solution.py:64
  94.2 9.3 %collective-permute-start.6 = (bf16[256,1152]{1,0:T(8,128)(2,1)S(1)}, bf16[256,1152]{1,0:T(8,128)(2,1)S(1)}, u32[]{:S(2)}, u32[]{:S(2)}) collective-permute-start(bf16[256,1152]{1,0:T(8,128)(2,1)S(1)} %collective-permute-done.4), channel_id=1, source_target_pairs={{0,1},{1,2},{2,3},{3,4},{4,5},{5,6},{6,7},{7,0},{8,9},{9,10},{10,1... | collective-permute-start | bytes 1769480 | tf_op jit(solution)/shard_map/ppermute | solution.py:59
Sparse Core Ops, SparseCore 0:
  113.7 132.8 all-gather.1
